TPU v7x, 32 devices: a whole 2x2x4 slice. The times are simulated.
32 devices in a mesh: gx: 2 (over core), ga: 4 (over y, x), gz: 4 (over z).
Axes of the slice: x: 2, y: 2, z: 4, core: 2. Of those that a mesh axis runs over, the one named last changes fastest.
Arguments:
- right_side: float32 [32, 64, 512], P('gx', 'ga', 'gz'), may hold values from -15 to 15
- diagonal: float32 [32, 64, 512], P('gx', 'ga', 'gz'), may hold values from 0.25 to 2
- basis_tables: float32 [3, 12, 12], replicated, may hold values from -1.75 to 1.75
- eigenvalues: float32 [3, 12], replicated, may hold values from 0.3 to 3
- coarse_blocks: float32 [2, 4, 4, 2, 64, 64], P('gx', 'ga', 'gz'), may hold values from -1 to 1
- coarse_columns: int32 [2, 4, 4, 2], P('gx', 'ga', 'gz'), may hold values from 0 to 15
Outputs:
- solution: float32 [32, 64, 512], P('gx', 'ga', 'gz')
- residual: float32 [32, 64, 512], P('gx', 'ga', 'gz')
All inputs are finite; a program needn't handle non-finite values.
Results may differ from a plain program's by a relative error of at most 0.0003.
Values sent between devices are 32-bit elements; how exact they have to be, the bound alone decides.
No kernel may reach another device: no remote copies, remote signals or barrier semaphores. Data moves between devices by JAX's collectives and lax.ppermute only.
A program may use at most 64 MiB of HBM per device.

v0:
```python
import jax
import jax.numpy as jnp
from jax import lax
from jax.sharding import PartitionSpec as P

PTS = 8
RIM = 2
WIDE = 12
CYCLES = 2
PRECISE = lax.Precision.HIGHEST


def padded_2(value, sides, width):
    for axis, dim in sides:
        size, length = (lax.axis_size(axis), value.shape[dim])
        up = [(i, (i + 1) % size) for i in range(size - 1)]
        down = [(j, i) for i, j in up]
        last = lax.slice_in_dim(value, length - width, length, axis=dim)
        leading = lax.slice_in_dim(value, 0, width, axis=dim)
        before = lax.ppermute(last, axis, up)
        after = lax.ppermute(leading, axis, down)
        value = jnp.concatenate([before, value, after], axis=dim)
    return value


def operate(field, diagonal):
    padded = padded_2(field, (("gx", 0), ("ga", 1), ("gz", 2)), 1)
    beside = padded[2:, 1:-1, 1:-1] + padded[:-2, 1:-1, 1:-1]
    beside = beside + padded[1:-1, 2:, 1:-1] + padded[1:-1, :-2, 1:-1]
    beside = beside + padded[1:-1, 1:-1, 2:] + padded[1:-1, 1:-1, :-2]
    return (6.0 + diagonal) * field - beside


def forward_table(count, basis):
    row_index = jnp.arange(PTS * count + 2 * RIM, dtype=jnp.int32)
    element = jnp.arange(count, dtype=jnp.int32)
    offset = jnp.arange(WIDE, dtype=jnp.int32)
    select = (
        row_index[:, None, None] == PTS * element[None, :, None] + offset[None, None, :]
    ).astype(jnp.float32)
    table = jnp.einsum("rcj,jm->rcm", select, basis, precision=PRECISE)
    return table.reshape(PTS * count + 2 * RIM, count * WIDE)


def backward_table(count, basis):
    same = jnp.eye(count, dtype=jnp.float32)
    table = jnp.einsum("cd,im->cmdi", same, basis[RIM : RIM + PTS], precision=PRECISE)
    return table.reshape(count * WIDE, count * PTS)


def schwarz_part(field, basis_tables, eigenvalues):
    count_x = field.shape[0] // PTS
    count_y = field.shape[1] // PTS
    count_z = field.shape[2] // PTS
    padded = padded_2(field, (("gx", 0), ("ga", 1), ("gz", 2)), RIM)
    spectral = jnp.einsum(
        "pqr,rc->pqc", padded, forward_table(count_z, basis_tables[2]), precision=PRECISE
    )
    spectral = jnp.einsum(
        "pqc,pa->aqc", spectral, forward_table(count_x, basis_tables[0]), precision=PRECISE
    )
    spectral = jnp.einsum(
        "aqc,qb->abc", spectral, forward_table(count_y, basis_tables[1]), precision=PRECISE
    )
    denominator = (
        jnp.tile(eigenvalues[0], count_x)[:, None, None]
        + jnp.tile(eigenvalues[1], count_y)[None, :, None]
    )
    denominator = denominator + jnp.tile(eigenvalues[2], count_z)[None, None, :]
    spectral = spectral / denominator
    local_part = jnp.einsum(
        "abc,cr->abr", spectral, backward_table(count_z, basis_tables[2]), precision=PRECISE
    )
    local_part = jnp.einsum(
        "abr,ap->pbr", local_part, backward_table(count_x, basis_tables[0]), precision=PRECISE
    )
    local_part = jnp.einsum(
        "pbr,bq->pqr", local_part, backward_table(count_y, basis_tables[1]), precision=PRECISE
    )
    return local_part


def coarse_part(field, blocks, selector):
    count_x = field.shape[0] // PTS
    count_y = field.shape[1] // PTS
    count_z = field.shape[2] // PTS
    cells = count_x * count_y * count_z
    means = jnp.mean(field.reshape(count_x, PTS, count_y, PTS, count_z, PTS), axis=(1, 3, 5))
    restricted = means.reshape(cells)
    terms = jnp.einsum("kpq,p->kq", blocks, restricted, precision=PRECISE)
    buffer = jnp.einsum("kj,kq->jq", selector, terms, precision=PRECISE)
    owned = lax.psum_scatter(buffer, ("ga", "gz"), scatter_dimension=0, tiled=True)
    whole = lax.all_gather(owned, ("ga", "gz"), axis=0, tiled=True)
    picked = jnp.dot(selector, whole, precision=PRECISE)
    coarse = jnp.einsum("kpq,kq->p", blocks, picked, precision=PRECISE)
    coarse = coarse.reshape(count_x, 1, count_y, 1, count_z, 1)
    spread = jnp.broadcast_to(coarse, (count_x, PTS, count_y, PTS, count_z, PTS))
    return spread.reshape(field.shape)


def start_norm(residual):
    return jnp.sqrt(lax.psum(jnp.sum(residual * residual), ("gx", "ga", "gz")))


def body(right_side, diagonal, basis_tables, eigenvalues, coarse_blocks, coarse_columns):
    blocks = coarse_blocks.reshape(coarse_blocks.shape[3:])
    columns = coarse_columns.reshape(coarse_columns.shape[3])
    group = lax.axis_size(("ga", "gz"))
    selector = (columns[:, None] == jnp.arange(group, dtype=jnp.int32)[None, :]).astype(jnp.float32)

    def precondition(field):
        return schwarz_part(field, basis_tables, eigenvalues) + coarse_part(field, blocks, selector)

    solution = jnp.zeros_like(right_side)
    residual = right_side
    for restart in range(CYCLES):
        initial_norm = start_norm(residual)
        first_vector = residual / initial_norm
        first_zed = precondition(first_vector)
        first_image = operate(first_zed, diagonal)
        first_proj, image_square = lax.psum(
            (jnp.sum(first_vector * first_image), jnp.sum(first_image * first_image)),
            ("gx", "ga", "gz"),
        )
        first_ortho = first_image - first_proj * first_vector
        first_len = jnp.sqrt(image_square - first_proj * first_proj)
        second_vector = first_ortho / first_len
        second_zed = precondition(second_vector)
        second_image = operate(second_zed, diagonal)
        upper_proj, lower_proj, second_square = lax.psum(
            (
                jnp.sum(first_vector * second_image),
                jnp.sum(second_vector * second_image),
                jnp.sum(second_image * second_image),
            ),
            ("gx", "ga", "gz"),
        )
        second_len = jnp.sqrt(second_square - upper_proj * upper_proj - lower_proj * lower_proj)
        gram_first = first_proj * first_proj + first_len * first_len
        gram_cross = first_proj * upper_proj + first_len * lower_proj
        gram_second = upper_proj * upper_proj + lower_proj * lower_proj + second_len * second_len
        target_first = initial_norm * first_proj
        target_second = initial_norm * upper_proj
        determinant = gram_first * gram_second - gram_cross * gram_cross
        weight_first = (gram_second * target_first - gram_cross * target_second) / determinant
        weight_second = (gram_first * target_second - gram_cross * target_first) / determinant
        solution = solution + weight_first * first_zed + weight_second * second_zed
        residual = right_side - operate(solution, diagonal)
    return (solution, residual)


def solution(mesh):
    in_specs = (
        P("gx", "ga", "gz"),
        P("gx", "ga", "gz"),
        P(),
        P(),
        P("gx", "ga", "gz", None, None, None),
        P("gx", "ga", "gz", None),
    )
    out_specs = (P("gx", "ga", "gz"), P("gx", "ga", "gz"))
    return jax.shard_map(body, mesh=mesh, in_specs=in_specs, out_specs=out_specs, check_vma=False)
```

profile of v0, /device:TPU:12, one launch (start us, length us, event | category | flops | bytes accessed | tf_op | source)
XLA Modules:
  0.0 856.3 jit_solution(14189468546565872897)
XLA Ops:
  2.2 41.6 %psum.84 = f32[]{:T(128)} all-reduce(f32[]{:T(128)} %multiply_reduce_fusion.11), channel_id=1, replica_groups=mesh['gx'=2,'ga'=4,'gz'=4] {'gx','ga','gz'}, use_global_device_ids=true, to_apply=%region_1.0 | all-reduce | flops 1 | bytes 8 | tf_op jit(solution)/shard_map/psum | solution.py:102
  50.8 37.9 %all-reduce = f32[16,64]{1,0:T(8,128)S(1)} all-reduce(f32[16,64]{1,0:T(8,128)S(1)} %fusion.102), channel_id=2, replica_groups=mesh['gx'=2,'ga'=4,'gz'=4] {'ga','gz'}, use_global_device_ids=true, to_apply=%region_3.0.clone | all-reduce | flops 1024 | bytes 8192
  90.0 38.2 %all-gather = f32[16,1,64]{2,1,0:T(1,128)S(1)} all-gather(f32[1,1,64]{2,1,0:T(1,128)S(1)} %fusion.103), channel_id=1, replica_groups=mesh['gx'=2,'ga'=4,'gz'=4] {'ga','gz'}, dimensions={0}, use_global_device_ids=true | all-gather | bytes 4352 | tf_op jit(solution)/shard_map/all_gather | solution.py:93
  131.2 4.8 collective-permute-start.3
  157.4 5.1 collective-permute-start.8
  181.8 38.4 %all-reduce.7 = (f32[]{:T(128)}, f32[]{:T(128)}) all-reduce(f32[]{:T(128)} %get-tuple-element.11, f32[]{:T(128)} %get-tuple-element.10), channel_id=1, replica_groups=mesh['gx'=2,'ga'=4,'gz'=4] {'gx','ga','gz'}, use_global_device_ids=true, to_apply=%region_7.0 | all-reduce | flops 2 | bytes 16 | tf_op jit(solution)/shard_map/psum | solution.py:121
  227.4 39.5 %all-reduce.1 = f32[16,64]{1,0:T(8,128)S(1)} all-reduce(f32[16,64]{1,0:T(8,128)S(1)} %fusion.100), channel_id=3, replica_groups=mesh['gx'=2,'ga'=4,'gz'=4] {'ga','gz'}, use_global_device_ids=true, to_apply=%region_9.0.clone | all-reduce | flops 1024 | bytes 8192
  267.5 37.8 %all-gather.1 = f32[16,1,64]{2,1,0:T(1,128)S(1)} all-gather(f32[1,1,64]{2,1,0:T(1,128)S(1)} %fusion.104), channel_id=1, replica_groups=mesh['gx'=2,'ga'=4,'gz'=4] {'ga','gz'}, dimensions={0}, use_global_device_ids=true | all-gather | bytes 4352 | tf_op jit(solution)/shard_map/all_gather | solution.py:93
  307.3 4.8 collective-permute-start.15
  334.5 5.1 collective-permute-start.20
  341.6 4.5 collective-permute-done.21
  359.0 38.5 %all-reduce.6 = (f32[]{:T(128)}, f32[]{:T(128)}, f32[]{:T(128)}) all-reduce(f32[]{:T(128)} %get-tuple-element.9, f32[]{:T(128)} %get-tuple-element.8, f32[]{:T(128)} %get-tuple-element.7), channel_id=1, replica_groups=mesh['gx'=2,'ga'=4,'gz'=4] {'gx','ga','gz'}, use_global_device_ids=true, to_apply=%region_11.0 | all-reduce | flops 3 | bytes 24 | tf_op jit(solution)/shard_map/psum | solution.py:130
  431.0 38.3 %psum.90 = f32[]{:T(128)} all-reduce(f32[]{:T(128)} %get-tuple-element.23), channel_id=1, replica_groups=mesh['gx'=2,'ga'=4,'gz'=4] {'gx','ga','gz'}, use_global_device_ids=true, to_apply=%region_17.0 | all-reduce | flops 1 | bytes 8 | tf_op jit(solution)/shard_map/psum | solution.py:102
  474.7 39.5 %all-reduce.2 = f32[16,64]{1,0:T(8,128)S(1)} all-reduce(f32[16,64]{1,0:T(8,128)S(1)} %fusion.98), channel_id=4, replica_groups=mesh['gx'=2,'ga'=4,'gz'=4] {'ga','gz'}, use_global_device_ids=true, to_apply=%region_19.0.clone | all-reduce | flops 1024 | bytes 8192
  514.8 37.8 %all-gather.2 = f32[16,1,64]{2,1,0:T(1,128)S(1)} all-gather(f32[1,1,64]{2,1,0:T(1,128)S(1)} %fusion.105), channel_id=1, replica_groups=mesh['gx'=2,'ga'=4,'gz'=4] {'ga','gz'}, dimensions={0}, use_global_device_ids=true | all-gather | bytes 4352 | tf_op jit(solution)/shard_map/all_gather | solution.py:93
  554.6 4.8 collective-permute-start.33
  581.9 5.1 collective-permute-start.38
  606.2 38.4 %all-reduce.5 = (f32[]{:T(128)}, f32[]{:T(128)}) all-reduce(f32[]{:T(128)} %get-tuple-element.6, f32[]{:T(128)} %get-tuple-element.5), channel_id=1, replica_groups=mesh['gx'=2,'ga'=4,'gz'=4] {'gx','ga','gz'}, use_global_device_ids=true, to_apply=%region_23.0 | all-reduce | flops 2 | bytes 16 | tf_op jit(solution)/shard_map/psum | solution.py:121
  651.9 39.5 %all-reduce.3 = f32[16,64]{1,0:T(8,128)S(1)} all-reduce(f32[16,64]{1,0:T(8,128)S(1)} %fusion.96), channel_id=5, replica_groups=mesh['gx'=2,'ga'=4,'gz'=4] {'ga','gz'}, use_global_device_ids=true, to_apply=%region_25.0.clone | all-reduce | flops 1024 | bytes 8192
  692.1 37.8 %all-gather.3 = f32[16,1,64]{2,1,0:T(1,128)S(1)} all-gather(f32[1,1,64]{2,1,0:T(1,128)S(1)} %fusion.106), channel_id=1, replica_groups=mesh['gx'=2,'ga'=4,'gz'=4] {'ga','gz'}, dimensions={0}, use_global_device_ids=true | all-gather | bytes 4352 | tf_op jit(solution)/shard_map/all_gather | solution.py:93
  731.8 4.8 collective-permute-start.45
  741.0 4.8 collective-permute-start.47
  759.4 5.1 collective-permute-start.50
  784.3 38.5 %all-reduce.4 = (f32[]{:T(128)}, f32[]{:T(128)}, f32[]{:T(128)}) all-reduce(f32[]{:T(128)} %get-tuple-element.4, f32[]{:T(128)} %get-tuple-element.3, f32[]{:T(128)} %get-tuple-element.2), channel_id=1, replica_groups=mesh['gx'=2,'ga'=4,'gz'=4] {'gx','ga','gz'}, use_global_device_ids=true, to_apply=%region_27.0 | all-reduce | flops 3 | bytes 24 | tf_op jit(solution)/shard_map/psum | solution.py:130
  (314 shorter events, 245.1 us)
Async XLA Ops:
  45.5 83.7 %collective-permute-start = (f32[2,16,128]{2,1,0:T(8,128)S(1)}, f32[2,16,128]{2,1,0:T(8,128)S(1)}, u32[]{:S(2)}, u32[]{:S(2)}) collective-permute-start(f32[2,16,128]{2,1,0:T(8,128)S(1)} %get-tuple-element.84), channel_id=1, source_target_pairs={{0,16},{1,17},{2,18},{3,19},{4,20},{5,21},{6,22},{7,23},{8,24},{9,... | collective-permute-start | bytes 49160 | tf_op jit(solution)/shard_map/ppermute | solution.py:20
  46.8 82.4 %collective-permute-start.1 = (f32[2,16,128]{2,1,0:T(8,128)S(1)}, f32[2,16,128]{2,1,0:T(8,128)S(1)}, u32[]{:S(2)}, u32[]{:S(2)}) collective-permute-start(f32[2,16,128]{2,1,0:T(8,128)S(1)} %get-tuple-element.85), channel_id=1, source_target_pairs={{16,0},{17,1},{18,2},{19,3},{20,4},{21,5},{22,6},{23,7},{24,8},{25... | collective-permute-start | bytes 49160 | tf_op jit(solution)/shard_map/ppermute | solution.py:21
  138.4 8.3 collective-permute-start.4
  140.3 8.3 collective-permute-start.5
  169.1 8.1 collective-permute-start.10
  173.1 7.9 collective-permute-start.11
  223.9 81.4 %collective-permute-start.12 = (f32[2,16,128]{2,1,0:T(8,128)S(1)}, f32[2,16,128]{2,1,0:T(8,128)S(1)}, u32[]{:S(2)}, u32[]{:S(2)}) collective-permute-start(f32[2,16,128]{2,1,0:T(8,128)S(1)} %get-tuple-element.80), channel_id=1, source_target_pairs={{0,16},{1,17},{2,18},{3,19},{4,20},{5,21},{6,22},{7,23},{8,24},{9,... | collective-permute-start | bytes 49160 | tf_op jit(solution)/shard_map/ppermute | solution.py:20
  225.3 80.0 %collective-permute-start.13 = (f32[2,16,128]{2,1,0:T(8,128)S(1)}, f32[2,16,128]{2,1,0:T(8,128)S(1)}, u32[]{:S(2)}, u32[]{:S(2)}) collective-permute-start(f32[2,16,128]{2,1,0:T(8,128)S(1)} %get-tuple-element.81), channel_id=1, source_target_pairs={{16,0},{17,1},{18,2},{19,3},{20,4},{21,5},{22,6},{23,7},{24,8},{25... | collective-permute-start | bytes 49160 | tf_op jit(solution)/shard_map/ppermute | solution.py:21
  314.5 8.3 collective-permute-start.16
  316.4 8.4 collective-permute-start.17
  346.3 8.1 collective-permute-start.22
  350.2 7.9 collective-permute-start.23
  418.3 8.1 collective-permute-start.28
  471.2 81.5 %collective-permute-start.30 = (f32[2,16,128]{2,1,0:T(8,128)S(1)}, f32[2,16,128]{2,1,0:T(8,128)S(1)}, u32[]{:S(2)}, u32[]{:S(2)}) collective-permute-start(f32[2,16,128]{2,1,0:T(8,128)S(1)} %get-tuple-element.74), channel_id=1, source_target_pairs={{0,16},{1,17},{2,18},{3,19},{4,20},{5,21},{6,22},{7,23},{8,24},{9,... | collective-permute-start | bytes 49160 | tf_op jit(solution)/shard_map/ppermute | solution.py:20
  472.6 80.0 %collective-permute-start.31 = (f32[2,16,128]{2,1,0:T(8,128)S(1)}, f32[2,16,128]{2,1,0:T(8,128)S(1)}, u32[]{:S(2)}, u32[]{:S(2)}) collective-permute-start(f32[2,16,128]{2,1,0:T(8,128)S(1)} %get-tuple-element.75), channel_id=1, source_target_pairs={{16,0},{17,1},{18,2},{19,3},{20,4},{21,5},{22,6},{23,7},{24,8},{25... | collective-permute-start | bytes 49160 | tf_op jit(solution)/shard_map/ppermute | solution.py:21
  561.8 8.3 collective-permute-start.34
  563.7 8.4 collective-permute-start.35
  593.6 8.1 collective-permute-start.40
  648.4 81.5 %collective-permute-start.42 = (f32[2,16,128]{2,1,0:T(8,128)S(1)}, f32[2,16,128]{2,1,0:T(8,128)S(1)}, u32[]{:S(2)}, u32[]{:S(2)}) collective-permute-start(f32[2,16,128]{2,1,0:T(8,128)S(1)} %get-tuple-element.70), channel_id=1, source_target_pairs={{0,16},{1,17},{2,18},{3,19},{4,20},{5,21},{6,22},{7,23},{8,24},{9,... | collective-permute-start | bytes 49160 | tf_op jit(solution)/shard_map/ppermute | solution.py:20
  649.9 80.0 %collective-permute-start.43 = (f32[2,16,128]{2,1,0:T(8,128)S(1)}, f32[2,16,128]{2,1,0:T(8,128)S(1)}, u32[]{:S(2)}, u32[]{:S(2)}) collective-permute-start(f32[2,16,128]{2,1,0:T(8,128)S(1)} %get-tuple-element.71), channel_id=1, source_target_pairs={{16,0},{17,1},{18,2},{19,3},{20,4},{21,5},{22,6},{23,7},{24,8},{25... | collective-permute-start | bytes 49160 | tf_op jit(solution)/shard_map/ppermute | solution.py:21
  739.0 8.4 collective-permute-start.46
  741.0 8.6 %collective-permute-start.47 = (f32[20,20,2]{2,1,0:T(8,128)}, f32[20,20,2]{2,1,0:T(8,128)}, u32[]{:S(2)}, u32[]{:S(2)}) collective-permute-start(f32[20,20,2]{2,1,0:T(8,128)} %get-tuple-element.27), channel_id=1, source_target_pairs={{1,0},{2,1},{3,2},{5,4},{6,5},{7,6},{9,8},{10,9},{11,10},{13,12},{... | collective-permute-start | bytes 9608 | tf_op jit(solution)/shard_map/ppermute | solution.py:21
  771.1 8.1 collective-permute-start.52
  843.3 8.1 collective-permute-start.58
  (62 other events, 663.4 us)
where the time goes:
time: 868 us; the launch traced here: 856 us
  blocking collectives  542 us (62%)
  starting transfers between devices  164 us (19%)
  waiting for transfers between devices  79 us (9%)
  between operations  20.5 us (2%)
  local copies, waits for them, and re-layouts  18.6 us (2%)
  matrix products  17.2 us (2%)
  other arithmetic  15.3 us (2%)
    unnamed x4, blocking collectives  156 us
    all_gather x4, blocking collectives, coarse_part(): whole = lax.all_gather(owned, ('ga', 'gz'), axis=0, tiled=True)  152 us
    ppermute x30, starting transfers between devices, padded_2(): after = lax.ppermute(leading, axis, down)  100 us
    psum x2, blocking collectives, start_norm(): return jnp.sqrt(lax.psum(jnp.sum(residual * residual), ('gx', 'ga', 'gz')))  79.9 us
    psum x2, blocking collectives, body(): lax.psum((jnp.sum(first_vector * second_image), jnp.sum(second_vector * s...  76.9 us
    psum x2, blocking collectives, body(): lax.psum((jnp.sum(first_vector * first_image), jnp.sum(first_image * firs...  76.8 us
    ppermute x30, starting transfers between devices, padded_2(): before = lax.ppermute(last, axis, up)  63.7 us
    ppermute x30, waiting for transfers between devices, padded_2(): before = lax.ppermute(last, axis, up)  54 us
  transfers between devices with their start and end apart: 60, of which 35 were waited for; matrix products, arithmetic and copies ran while one was open for 2% of the time, Pallas kernels for 0%

commit v1 on v0

--- a/solution.py
+++ b/solution.py
@@ -8,6 +8,19 @@
 WIDE = 12
 CYCLES = 2
 PRECISE = lax.Precision.HIGHEST
+
+
+def gather_around(x, axis, dim):
+    ways = lax.axis_size(axis)
+    up = [(d, (d + 1) % ways) for d in range(ways)]
+    down = [(d, (d - 1) % ways) for d in range(ways)]
+    earlier, later = ([x], [x])
+    for _ in range(ways // 2):
+        earlier.append(lax.ppermute(earlier[-1], axis, up))
+    for _ in range((ways - 1) // 2):
+        later.append(lax.ppermute(later[-1], axis, down))
+    line = jnp.concatenate([*earlier[::-1], *later[1:]], axis=dim)
+    return jnp.roll(line, (lax.axis_index(axis) - ways // 2) * x.shape[dim], axis=dim)
 
 
 def padded_2(value, sides, width):
@@ -90,7 +103,7 @@
     terms = jnp.einsum("kpq,p->kq", blocks, restricted, precision=PRECISE)
     buffer = jnp.einsum("kj,kq->jq", selector, terms, precision=PRECISE)
     owned = lax.psum_scatter(buffer, ("ga", "gz"), scatter_dimension=0, tiled=True)
-    whole = lax.all_gather(owned, ("ga", "gz"), axis=0, tiled=True)
+    whole = gather_around(owned, ("ga", "gz"), 0)
     picked = jnp.dot(selector, whole, precision=PRECISE)
     coarse = jnp.einsum("kpq,kq->p", blocks, picked, precision=PRECISE)
     coarse = coarse.reshape(count_x, 1, count_y, 1, count_z, 1)

time: 868 us -> 945 us (1.089)
  starting transfers between devices: 164 us -> 322 us
  blocking collectives: 542 us -> 391 us
  waiting for transfers between devices: 79 us -> 148 us
    all_gather x4 -> x0, blocking collectives: 152 us -> none  [coarse_part(): whole = lax.all_gather(owned, ('ga', 'gz'), axis=0, tiled=True)]
    ppermute x0 -> x60, starting transfers between devices: none -> 146 us  [the longest x28 146 us: gather_around(): later.append(lax.ppermute(later[-1], axis, down))]
    ppermute x0 -> x60, waiting for transfers between devices: none -> 68 us  [the longest x32 67.6 us: gather_around(): earlier.append(lax.ppermute(earlier[-1], axis, up))]
    ppermute x30, starting transfers between devices: 100 us -> 112 us  [padded_2(): after = lax.ppermute(leading, axis, down)]
  transfers between devices with their start and end apart: 60 -> 120, of which waited for: 35 -> 68; matrix products, arithmetic and copies ran while one was open for 2% -> 1% of each run, Pallas kernels for 0% -> 0%
where the time goes in v1:
time: 945 us; the launch traced here: 934 us
  blocking collectives  391 us (41%)
  starting transfers between devices  322 us (34%)
  waiting for transfers between devices  148 us (16%)
  between operations  21.2 us (2%)
  local copies, waits for them, and re-layouts  19.3 us (2%)
  matrix products  17.2 us (2%)
  other arithmetic  16.1 us (2%)
    unnamed x4, blocking collectives  156 us
    ppermute x28, starting transfers between devices, gather_around(): later.append(lax.ppermute(later[-1], axis, down))  146 us
    ppermute x30, starting transfers between devices, padded_2(): after = lax.ppermute(leading, axis, down)  112 us
    psum x2, blocking collectives, start_norm(): return jnp.sqrt(lax.psum(jnp.sum(residual * residual), ('gx', 'ga', 'gz')))  80.1 us
    psum x2, blocking collectives, body(): lax.psum((jnp.sum(first_vector * first_image), jnp.sum(first_image * firs...  77.2 us
    psum x2, blocking collectives, body(): lax.psum((jnp.sum(first_vector * second_image), jnp.sum(second_vector * s...  77 us
    ppermute x32, waiting for transfers between devices, gather_around(): earlier.append(lax.ppermute(earlier[-1], axis, up))  67.6 us
    ppermute x30, starting transfers between devices, padded_2(): before = lax.ppermute(last, axis, up)  63.7 us
  transfers between devices with their start and end apart: 120, of which 68 were waited for; matrix products, arithmetic and copies ran while one was open for 1% of the time, Pallas kernels for 0%

profile of v1, /device:TPU:12, one launch (start us, length us, event | category | flops | bytes accessed | tf_op | source)
XLA Modules:
  0.0 934.2 jit_solution(6014687145433446364)
XLA Ops:
  2.2 41.6 %psum.84 = f32[]{:T(128)} all-reduce(f32[]{:T(128)} %multiply_reduce_fusion.11), channel_id=1, replica_groups=mesh['gx'=2,'ga'=4,'gz'=4] {'gx','ga','gz'}, use_global_device_ids=true, to_apply=%region_1.0 | all-reduce | flops 1 | bytes 8 | tf_op jit(solution)/shard_map/psum | solution.py:115
  47.4 37.9 %all-reduce = f32[16,64]{1,0:T(8,128)S(1)} all-reduce(f32[16,64]{1,0:T(8,128)S(1)} %fusion.114), channel_id=2, replica_groups=mesh['gx'=2,'ga'=4,'gz'=4] {'ga','gz'}, use_global_device_ids=true, to_apply=%region_3.0.clone | all-reduce | flops 1024 | bytes 8192
  122.3 5.7 collective-permute-start.19
  130.1 5.7 collective-permute-start.20
  137.0 6.7 collective-permute-done.13
  154.8 6.9 collective-permute-start.5
  199.3 38.9 %all-reduce.7 = (f32[]{:T(128)}, f32[]{:T(128)}) all-reduce(f32[]{:T(128)} %get-tuple-element.12, f32[]{:T(128)} %get-tuple-element.11), channel_id=1, replica_groups=mesh['gx'=2,'ga'=4,'gz'=4] {'gx','ga','gz'}, use_global_device_ids=true, to_apply=%region_7.9 | all-reduce | flops 2 | bytes 16 | tf_op jit(solution)/shard_map/psum | solution.py:134
  245.4 39.5 %all-reduce.1 = f32[16,64]{1,0:T(8,128)S(1)} all-reduce(f32[16,64]{1,0:T(8,128)S(1)} %fusion.113), channel_id=3, replica_groups=mesh['gx'=2,'ga'=4,'gz'=4] {'ga','gz'}, use_global_device_ids=true, to_apply=%region_9.11.clone | all-reduce | flops 1024 | bytes 8192
  332.5 7.1 collective-permute-done.40
  350.7 6.9 collective-permute-start.32
  396.3 38.5 %all-reduce.6 = (f32[]{:T(128)}, f32[]{:T(128)}, f32[]{:T(128)}) all-reduce(f32[]{:T(128)} %get-tuple-element.10, f32[]{:T(128)} %get-tuple-element.9, f32[]{:T(128)} %get-tuple-element.8), channel_id=1, replica_groups=mesh['gx'=2,'ga'=4,'gz'=4] {'gx','ga','gz'}, use_global_device_ids=true, to_apply=%region_11.13 | all-reduce | flops 3 | bytes 24 | tf_op jit(solution)/shard_map/psum | solution.py:143
  468.4 38.5 %psum.90 = f32[]{:T(128)} all-reduce(f32[]{:T(128)} %get-tuple-element.24), channel_id=1, replica_groups=mesh['gx'=2,'ga'=4,'gz'=4] {'gx','ga','gz'}, use_global_device_ids=true, to_apply=%region_17.19 | all-reduce | flops 1 | bytes 8 | tf_op jit(solution)/shard_map/psum | solution.py:115
  512.3 39.5 %all-reduce.2 = f32[16,64]{1,0:T(8,128)S(1)} all-reduce(f32[16,64]{1,0:T(8,128)S(1)} %fusion.112), channel_id=4, replica_groups=mesh['gx'=2,'ga'=4,'gz'=4] {'ga','gz'}, use_global_device_ids=true, to_apply=%region_19.21.clone | all-reduce | flops 1024 | bytes 8192
  599.4 7.1 collective-permute-done.73
  619.0 6.9 collective-permute-start.65
  664.4 38.4 %all-reduce.5 = (f32[]{:T(128)}, f32[]{:T(128)}) all-reduce(f32[]{:T(128)} %get-tuple-element.7, f32[]{:T(128)} %get-tuple-element.6), channel_id=1, replica_groups=mesh['gx'=2,'ga'=4,'gz'=4] {'gx','ga','gz'}, use_global_device_ids=true, to_apply=%region_23.25 | all-reduce | flops 2 | bytes 16 | tf_op jit(solution)/shard_map/psum | solution.py:134
  710.2 39.5 %all-reduce.3 = f32[16,64]{1,0:T(8,128)S(1)} all-reduce(f32[16,64]{1,0:T(8,128)S(1)} %fusion.111), channel_id=5, replica_groups=mesh['gx'=2,'ga'=4,'gz'=4] {'ga','gz'}, use_global_device_ids=true, to_apply=%region_25.27.clone | all-reduce | flops 1024 | bytes 8192
  761.5 5.8 collective-permute-start.103
  768.7 5.6 collective-permute-start.104
  775.8 5.6 collective-permute-start.105
  782.9 5.6 collective-permute-start.106
  797.2 7.1 collective-permute-done.100
  815.5 7.6 collective-permute-start.92
  861.8 38.5 %all-reduce.4 = (f32[]{:T(128)}, f32[]{:T(128)}, f32[]{:T(128)}) all-reduce(f32[]{:T(128)} %get-tuple-element.5, f32[]{:T(128)} %get-tuple-element.4, f32[]{:T(128)} %get-tuple-element.3), channel_id=1, replica_groups=mesh['gx'=2,'ga'=4,'gz'=4] {'gx','ga','gz'}, use_global_device_ids=true, to_apply=%region_27.29 | all-reduce | flops 3 | bytes 24 | tf_op jit(solution)/shard_map/psum | solution.py:143
  (416 shorter events, 431.9 us)
Async XLA Ops:
  89.7 54.1 %collective-permute-start = (f32[2,16,128]{2,1,0:T(8,128)S(1)}, f32[2,16,128]{2,1,0:T(8,128)S(1)}, u32[]{:S(2)}, u32[]{:S(2)}) collective-permute-start(f32[2,16,128]{2,1,0:T(8,128)S(1)} %get-tuple-element.85), channel_id=1, source_target_pairs={{0,16},{1,17},{2,18},{3,19},{4,20},{5,21},{6,22},{7,23},{8,24},{9,... | collective-permute-start | bytes 49160 | tf_op jit(solution)/shard_map/ppermute | solution.py:33
  90.9 52.8 %collective-permute-start.1 = (f32[2,16,128]{2,1,0:T(8,128)S(1)}, f32[2,16,128]{2,1,0:T(8,128)S(1)}, u32[]{:S(2)}, u32[]{:S(2)}) collective-permute-start(f32[2,16,128]{2,1,0:T(8,128)S(1)} %get-tuple-element.86), channel_id=1, source_target_pairs={{16,0},{17,1},{18,2},{19,3},{20,4},{21,5},{22,6},{23,7},{24,8},{25... | collective-permute-start | bytes 49160 | tf_op jit(solution)/shard_map/ppermute | solution.py:34
  152.9 11.3 %collective-permute-start.4 = (f32[20,20,2]{2,1,0:T(8,128)}, f32[20,20,2]{2,1,0:T(8,128)S(1)}, u32[]{:S(2)}, u32[]{:S(2)}) collective-permute-start(f32[20,20,2]{2,1,0:T(8,128)} %get-tuple-element.33), channel_id=1, source_target_pairs={{0,1},{1,2},{2,3},{4,5},{5,6},{6,7},{8,9},{9,10},{10,11},{12,13},{... | collective-permute-start | bytes 9608 | tf_op jit(solution)/shard_map/ppermute | solution.py:33
  154.8 10.9 %collective-permute-start.5 = (f32[20,20,2]{2,1,0:T(8,128)}, f32[20,20,2]{2,1,0:T(8,128)S(1)}, u32[]{:S(2)}, u32[]{:S(2)}) collective-permute-start(f32[20,20,2]{2,1,0:T(8,128)} %get-tuple-element.34), channel_id=1, source_target_pairs={{1,0},{2,1},{3,2},{5,4},{6,5},{7,6},{9,8},{10,9},{11,10},{13,12},{... | collective-permute-start | bytes 9608 | tf_op jit(solution)/shard_map/ppermute | solution.py:34
  186.3 8.1 collective-permute-start.25
  190.6 7.9 collective-permute-start.26
  241.9 97.7 %collective-permute-start.27 = (f32[2,16,128]{2,1,0:T(8,128)S(1)}, f32[2,16,128]{2,1,0:T(8,128)S(1)}, u32[]{:S(2)}, u32[]{:S(2)}) collective-permute-start(f32[2,16,128]{2,1,0:T(8,128)S(1)} %get-tuple-element.81), channel_id=1, source_target_pairs={{0,16},{1,17},{2,18},{3,19},{4,20},{5,21},{6,22},{7,23},{8,24},{9,... | collective-permute-start | bytes 49160 | tf_op jit(solution)/shard_map/ppermute | solution.py:33
  243.4 96.3 %collective-permute-start.28 = (f32[2,16,128]{2,1,0:T(8,128)S(1)}, f32[2,16,128]{2,1,0:T(8,128)S(1)}, u32[]{:S(2)}, u32[]{:S(2)}) collective-permute-start(f32[2,16,128]{2,1,0:T(8,128)S(1)} %get-tuple-element.82), channel_id=1, source_target_pairs={{16,0},{17,1},{18,2},{19,3},{20,4},{21,5},{22,6},{23,7},{24,8},{25... | collective-permute-start | bytes 49160 | tf_op jit(solution)/shard_map/ppermute | solution.py:34
  348.8 11.3 %collective-permute-start.31 = (f32[20,20,2]{2,1,0:T(8,128)}, f32[20,20,2]{2,1,0:T(8,128)S(1)}, u32[]{:S(2)}, u32[]{:S(2)}) collective-permute-start(f32[20,20,2]{2,1,0:T(8,128)} %get-tuple-element.31), channel_id=1, source_target_pairs={{0,1},{1,2},{2,3},{4,5},{5,6},{6,7},{8,9},{9,10},{10,11},{12,13},{... | collective-permute-start | bytes 9608 | tf_op jit(solution)/shard_map/ppermute | solution.py:33
  350.7 11.3 %collective-permute-start.32 = (f32[20,20,2]{2,1,0:T(8,128)}, f32[20,20,2]{2,1,0:T(8,128)}, u32[]{:S(2)}, u32[]{:S(2)}) collective-permute-start(f32[20,20,2]{2,1,0:T(8,128)} %get-tuple-element.32), channel_id=1, source_target_pairs={{1,0},{2,1},{3,2},{5,4},{6,5},{7,6},{9,8},{10,9},{11,10},{13,12},{... | collective-permute-start | bytes 9608 | tf_op jit(solution)/shard_map/ppermute | solution.py:34
  383.1 8.1 collective-permute-start.52
  387.5 7.9 collective-permute-start.53
  455.7 8.1 collective-permute-start.58
  508.8 97.7 %collective-permute-start.60 = (f32[2,16,128]{2,1,0:T(8,128)S(1)}, f32[2,16,128]{2,1,0:T(8,128)S(1)}, u32[]{:S(2)}, u32[]{:S(2)}) collective-permute-start(f32[2,16,128]{2,1,0:T(8,128)S(1)} %get-tuple-element.75), channel_id=1, source_target_pairs={{0,16},{1,17},{2,18},{3,19},{4,20},{5,21},{6,22},{7,23},{8,24},{9,... | collective-permute-start | bytes 49160 | tf_op jit(solution)/shard_map/ppermute | solution.py:33
  510.2 96.3 %collective-permute-start.61 = (f32[2,16,128]{2,1,0:T(8,128)S(1)}, f32[2,16,128]{2,1,0:T(8,128)S(1)}, u32[]{:S(2)}, u32[]{:S(2)}) collective-permute-start(f32[2,16,128]{2,1,0:T(8,128)S(1)} %get-tuple-element.76), channel_id=1, source_target_pairs={{16,0},{17,1},{18,2},{19,3},{20,4},{21,5},{22,6},{23,7},{24,8},{25... | collective-permute-start | bytes 49160 | tf_op jit(solution)/shard_map/ppermute | solution.py:34
  617.0 11.3 %collective-permute-start.64 = (f32[20,20,2]{2,1,0:T(8,128)}, f32[20,20,2]{2,1,0:T(8,128)S(1)}, u32[]{:S(2)}, u32[]{:S(2)}) collective-permute-start(f32[20,20,2]{2,1,0:T(8,128)} %get-tuple-element.29), channel_id=1, source_target_pairs={{0,1},{1,2},{2,3},{4,5},{5,6},{6,7},{8,9},{9,10},{10,11},{12,13},{... | collective-permute-start | bytes 9608 | tf_op jit(solution)/shard_map/ppermute | solution.py:33
  619.0 11.3 %collective-permute-start.65 = (f32[20,20,2]{2,1,0:T(8,128)}, f32[20,20,2]{2,1,0:T(8,128)}, u32[]{:S(2)}, u32[]{:S(2)}) collective-permute-start(f32[20,20,2]{2,1,0:T(8,128)} %get-tuple-element.30), channel_id=1, source_target_pairs={{1,0},{2,1},{3,2},{5,4},{6,5},{7,6},{9,8},{10,9},{11,10},{13,12},{... | collective-permute-start | bytes 9608 | tf_op jit(solution)/shard_map/ppermute | solution.py:34
  651.3 8.1 collective-permute-start.85
  706.7 97.7 %collective-permute-start.87 = (f32[2,16,128]{2,1,0:T(8,128)S(1)}, f32[2,16,128]{2,1,0:T(8,128)S(1)}, u32[]{:S(2)}, u32[]{:S(2)}) collective-permute-start(f32[2,16,128]{2,1,0:T(8,128)S(1)} %get-tuple-element.71), channel_id=1, source_target_pairs={{0,16},{1,17},{2,18},{3,19},{4,20},{5,21},{6,22},{7,23},{8,24},{9,... | collective-permute-start | bytes 49160 | tf_op jit(solution)/shard_map/ppermute | solution.py:33
  708.1 96.3 %collective-permute-start.88 = (f32[2,16,128]{2,1,0:T(8,128)S(1)}, f32[2,16,128]{2,1,0:T(8,128)S(1)}, u32[]{:S(2)}, u32[]{:S(2)}) collective-permute-start(f32[2,16,128]{2,1,0:T(8,128)S(1)} %get-tuple-element.72), channel_id=1, source_target_pairs={{16,0},{17,1},{18,2},{19,3},{20,4},{21,5},{22,6},{23,7},{24,8},{25... | collective-permute-start | bytes 49160 | tf_op jit(solution)/shard_map/ppermute | solution.py:34
  813.5 11.4 %collective-permute-start.91 = (f32[20,20,2]{2,1,0:T(8,128)}, f32[20,20,2]{2,1,0:T(8,128)}, u32[]{:S(2)}, u32[]{:S(2)}) collective-permute-start(f32[20,20,2]{2,1,0:T(8,128)} %get-tuple-element.27), channel_id=1, source_target_pairs={{0,1},{1,2},{2,3},{4,5},{5,6},{6,7},{8,9},{9,10},{10,11},{12,13},{... | collective-permute-start | bytes 9608 | tf_op jit(solution)/shard_map/ppermute | solution.py:33
  815.5 11.6 %collective-permute-start.92 = (f32[20,20,2]{2,1,0:T(8,128)}, f32[20,20,2]{2,1,0:T(8,128)}, u32[]{:S(2)}, u32[]{:S(2)}) collective-permute-start(f32[20,20,2]{2,1,0:T(8,128)} %get-tuple-element.28), channel_id=1, source_target_pairs={{1,0},{2,1},{3,2},{5,4},{6,5},{7,6},{9,8},{10,9},{11,10},{13,12},{... | collective-permute-start | bytes 9608 | tf_op jit(solution)/shard_map/ppermute | solution.py:34
  848.6 8.1 collective-permute-start.112
  921.2 8.1 collective-permute-start.118
  (113 other events, 1457.2 us)
